TPU v7x, 128 devices: a whole 4x4x4 slice. The times are simulated.
128 devices in a mesh: shard: 8 (over x, core), tensor: 16 (over z, y).
Axes of the slice: x: 4, y: 4, z: 4, core: 2. Of those that a mesh axis runs over, the one named last changes fastest.
Arguments:
- grad_square: bfloat16 [8, 768, 768], P(None, 'shard'), may hold values from -64 to 64
- grad_wide: bfloat16 [8, 2048, 768], P(None, 'shard'), may hold values from -64 to 64
- moment_square: float32 [8, 589824], P(None, ('shard', 'tensor')), may hold values from -6 to 6
- moment_wide: float32 [8, 1572864], P(None, ('shard', 'tensor')), may hold values from -6 to 6
Outputs:
- update_square: float32 [8, 768, 768], P(None, 'shard')
- update_wide: float32 [8, 2048, 768], P(None, 'shard')
- new_moment_square: float32 [8, 589824], P(None, ('shard', 'tensor'))
- new_moment_wide: float32 [8, 1572864], P(None, ('shard', 'tensor'))
All inputs are finite; a program needn't handle non-finite values.
Results may differ from a plain program's by a relative error of at most 0.0003.
Values sent between devices are 32-bit elements; how exact they have to be, the bound alone decides.
No kernel may reach another device: no remote copies, remote signals or barrier semaphores. Data moves between devices by JAX's collectives and lax.ppermute only.
A program may use at most 128 MiB of HBM per device.

v0:
```python
import math
import jax
import jax.numpy as jnp
from jax import lax
from jax.sharding import PartitionSpec as P

D = 768
FF = 2048
ITERS = 3
coef_a = 3.4445
coef_b = -4.775
coef_c = 2.0315
momentum_decay = 0.95
epsilon = 1e-07


def polynomial(row_gram, whole_gram):
    square_part = jnp.einsum(
        "mcd,mde->mce",
        row_gram,
        whole_gram,
        precision=lax.Precision.HIGHEST,
        preferred_element_type=jnp.float32,
    )
    return coef_b * row_gram + coef_c * square_part


def next_iterate(current, mixer):
    product = jnp.einsum(
        "mrc,mcd->mrd",
        current,
        mixer,
        precision=lax.Precision.HIGHEST,
        preferred_element_type=jnp.float32,
    )
    return coef_a * current + product


def partial_gram(current):
    return jnp.einsum(
        "mrc,mrd->mcd",
        current,
        current,
        precision=lax.Precision.HIGHEST,
        preferred_element_type=jnp.float32,
    )


def squares(values):
    return jnp.sum(values * values, axis=(1, 2))


def normalize(values, totals):
    return values / (jnp.sqrt(totals) + epsilon)[:, None, None]


def own_rows(grad, member, tensor_count):
    row_piece = grad.shape[1] // tensor_count
    return lax.dynamic_slice_in_dim(grad, member * row_piece, row_piece, 1)


def shards(grad_square, grad_wide, moment_square, moment_wide):
    tensor_count = lax.axis_size("tensor")
    member = lax.axis_index("tensor")
    flat_square = own_rows(grad_square, member, tensor_count).astype(jnp.float32)
    flat_wide = own_rows(grad_wide, member, tensor_count).astype(jnp.float32)
    new_square = momentum_decay * moment_square.reshape(flat_square.shape) + flat_square
    new_wide = momentum_decay * moment_wide.reshape(flat_wide.shape) + flat_wide
    look_square = flat_square + momentum_decay * new_square
    look_wide = flat_wide + momentum_decay * new_wide
    total_square, total_wide = lax.psum(
        (squares(look_square), squares(look_wide)), ("shard", "tensor")
    )
    start_square = normalize(look_square, total_square)
    start_wide = normalize(look_wide, total_wide)
    held_square, held_wide = (
        lax.all_to_all(start_square, "shard", split_axis=0, concat_axis=1, tiled=True),
        lax.all_to_all(start_wide, "shard", split_axis=0, concat_axis=1, tiled=True),
    )
    for iteration in range(ITERS):
        part_square = partial_gram(held_square)
        part_wide = partial_gram(held_wide)
        gram_square, gram_wide = lax.psum((part_square, part_wide), "tensor")
        mixer_square = polynomial(gram_square, gram_square)
        mixer_wide = polynomial(gram_wide, gram_wide)
        held_square = next_iterate(held_square, mixer_square)
        held_wide = next_iterate(held_wide, mixer_wide)
    scaled_square = math.sqrt(D) * held_square
    scaled_wide = math.sqrt(FF) * held_wide
    back_square, back_wide = (
        lax.all_to_all(scaled_square, "shard", split_axis=1, concat_axis=0, tiled=True),
        lax.all_to_all(scaled_wide, "shard", split_axis=1, concat_axis=0, tiled=True),
    )
    update_square, update_wide = (
        lax.all_gather(back_square, "tensor", axis=1, tiled=True),
        lax.all_gather(back_wide, "tensor", axis=1, tiled=True),
    )
    return (
        update_square,
        update_wide,
        new_square.reshape(moment_square.shape),
        new_wide.reshape(moment_wide.shape),
    )


def solution(mesh):
    return jax.shard_map(
        shards,
        mesh=mesh,
        in_specs=(
            P(None, "shard", None),
            P(None, "shard", None),
            P(None, ("shard", "tensor")),
            P(None, ("shard", "tensor")),
        ),
        out_specs=(
            P(None, "shard", None),
            P(None, "shard", None),
            P(None, ("shard", "tensor")),
            P(None, ("shard", "tensor")),
        ),
        check_vma=False,
    )
```

profile of v0, /device:TPU:1, one launch (start us, length us, event | category | flops | bytes accessed | tf_op | source)
XLA Modules:
  0.0 619.9 jit_solution(17534331259739057778)
XLA Ops:
  11.3 68.6 %all-reduce = (f32[8]{0:T(128)S(1)}, f32[8]{0:T(128)S(1)}) all-reduce(f32[8]{0:T(128)S(1)} %get-tuple-element.23, f32[8]{0:T(128)S(1)} %multiply_reduce_fusion), channel_id=1, replica_groups=mesh['shard'=8,'tensor'=16] {'shard','tensor'}, use_global_device_ids=true, to_apply=%region_1.0 | all-reduce | flops 16 | bytes 128 | tf_op jit(solution)/shard_map/psum | solution.py:71
  80.7 4.2 all-to-all-start
  84.9 2.0 fusion.78
  86.9 3.9 all-to-all-done
  90.8 4.3 all-to-all-start.2
  95.1 3.5 convolution_bitcast_fusion
  98.6 4.3 all-to-all-done.2
  102.9 3.5 convolution_bitcast_fusion.3
  106.6 105.0 %all-reduce.12.cloned.1.call-done = (f32[1,768,768]{2,1,0:T(8,128)}, f32[1,768,768]{2,1,0:T(8,128)}) async-done(((f32[1,768,768]{2,1,0:T(8,128)}, f32[1,768,768]{2,1,0:T(8,128)}), (f32[1,768,768]{2,1,0:T(8,128)}, f32[1,768,768]{2,1,0:T(8,128)})) %all-reduce.12.cloned.1.call-update) | async-done | bytes 4718608 | tf_op jit(solution)/shard_map/psum | solution.py:83
  211.6 8.5 %fusion.22 = f32[768,768]{1,0:T(8,128)S(1)} fusion(f32[1,768,768]{2,1,0:T(8,128)} %get-tuple-element.18), kind=kOutput, calls=%fused_computation.28 | convolution fusion | flops 5435817984 | bytes 4718592 | tf_op jit(solution)/shard_map/mcd,mde->mce/dot_general | solution.py:18
  220.1 1.8 fusion.63
  221.9 3.5 convolution_bitcast_fusion.5
  225.4 6.4 %fusion.10 = f32[768,768]{1,0:T(8,128)S(1)} fusion(f32[1,768,768]{2,1,0:T(8,128)S(1)} %copy-done.6), kind=kOutput, calls=%fused_computation.13 | convolution fusion | flops 5435817984 | bytes 4718592 | tf_op jit(solution)/shard_map/mcd,mde->mce/dot_general | solution.py:18
  233.4 3.5 convolution_bitcast_fusion.2
  237.0 108.1 %all-reduce.10.cloned.1.call-done = (f32[1,768,768]{2,1,0:T(8,128)}, f32[1,768,768]{2,1,0:T(8,128)}) async-done(((f32[1,768,768]{2,1,0:T(8,128)}, f32[1,768,768]{2,1,0:T(8,128)}), (f32[1,768,768]{2,1,0:T(8,128)}, f32[1,768,768]{2,1,0:T(8,128)})) %all-reduce.10.cloned.1.call-update) | async-done | bytes 4718608 | tf_op jit(solution)/shard_map/psum | solution.py:83
  345.1 8.5 %fusion.18 = f32[768,768]{1,0:T(8,128)S(1)} fusion(f32[1,768,768]{2,1,0:T(8,128)} %get-tuple-element.16), kind=kOutput, calls=%fused_computation.23 | convolution fusion | flops 5435817984 | bytes 4718592 | tf_op jit(solution)/shard_map/mcd,mde->mce/dot_general | solution.py:18
  353.6 1.8 fusion.66
  355.4 3.5 convolution_bitcast_fusion.4
  358.8 6.1 fusion.6
  365.0 1.7 fusion.39
  366.7 3.5 convolution_bitcast_fusion.1
  370.2 108.1 %all-reduce.8.cloned.1.call-done = (f32[1,768,768]{2,1,0:T(8,128)}, f32[1,768,768]{2,1,0:T(8,128)}) async-done(((f32[1,768,768]{2,1,0:T(8,128)}, f32[1,768,768]{2,1,0:T(8,128)}), (f32[1,768,768]{2,1,0:T(8,128)}, f32[1,768,768]{2,1,0:T(8,128)})) %all-reduce.8.cloned.1.call-update) | async-done | bytes 4718608 | tf_op jit(solution)/shard_map/psum | solution.py:83
  478.3 8.5 %fusion.14 = f32[768,768]{1,0:T(8,128)S(1)} fusion(f32[1,768,768]{2,1,0:T(8,128)} %get-tuple-element.14), kind=kOutput, calls=%fused_computation.18 | convolution fusion | flops 5435817984 | bytes 4718592 | tf_op jit(solution)/shard_map/mcd,mde->mce/dot_general | solution.py:18
  486.9 1.8 fusion.75
  488.8 10.3 %all_to_all.48 = f32[1,48,768]{2,0,1:T(1,128)S(1)} all-to-all(f32[1,48,768]{2,0,1:T(1,128)S(1)} %copy.19), channel_id=1, replica_groups=mesh['shard'=8,'tensor'=16] {'shard'}, dimensions={1} | all-to-all | bytes 294912 | tf_op jit(solution)/shard_map/all_to_all | solution.py:91
  500.5 6.0 fusion.2
  506.4 1.8 fusion.48
  508.6 11.3 %all_to_all.49 = f32[1,128,768]{2,0,1:T(1,128)S(1)} all-to-all(f32[1,128,768]{2,0,1:T(1,128)S(1)} %copy.21), channel_id=1, replica_groups=mesh['shard'=8,'tensor'=16] {'shard'}, dimensions={1} | all-to-all | bytes 786432 | tf_op jit(solution)/shard_map/all_to_all | solution.py:92
  521.7 21.0 %all-gather.3.cloned.1.call-done = f32[8,96,768]{2,0,1:T(8,128)} async-done(((f32[8,6,768]{2,0,1:T(8,128)}), f32[8,96,768]{2,0,1:T(8,128)}) %all-gather.3.cloned.1.call-update) | async-done | bytes 2359312 | tf_op jit(solution)/shard_map/all_gather | solution.py:95
  542.7 3.8 copy.22
  546.5 60.6 %all-gather.5.cloned.1.call-done = f32[8,256,768]{2,1,0:T(8,128)} async-done(((f32[8,16,768]{2,1,0:T(8,128)}), f32[8,256,768]{2,1,0:T(8,128)}) %all-gather.5.cloned.1.call-update) | async-done | bytes 6291472 | tf_op jit(solution)/shard_map/all_gather | solution.py:96
  607.1 6.0 copy.51
  (45 shorter events, 10.7 us)
Async XLA Ops:
  7.2 2.1 copy-start
  80.7 10.1 %all-to-all-start = ((f32[8,6,768]{2,1,0:T(8,128)}), f32[8,6,768]{2,1,0:T(8,128)S(1)}, u32[]{:S(2)}, u32[]{:S(2)}) async-start(f32[8,6,768]{2,1,0:T(8,128)} %copy.18), calls=%async_computation | async-start | bytes 393216 | tf_op jit(solution)/shard_map/all_to_all | solution.py:77
  90.8 12.0 %all-to-all-start.2 = ((f32[8,16,768]{2,1,0:T(8,128)}), f32[8,16,768]{2,1,0:T(8,128)S(1)}, u32[]{:S(2)}, u32[]{:S(2)}) async-start(f32[8,16,768]{2,1,0:T(8,128)} %get-tuple-element.21), calls=%async_computation.2 | async-start | bytes 786432 | tf_op jit(solution)/shard_map/all_to_all | solution.py:78
  95.1 116.4 %all-reduce.12.cloned.1.call-start = ((), (), s32[]{:S(2)}) async-start(), calls=%async_computation.8 | async-start | bytes 9437184 | tf_op jit(solution)/shard_map/psum | solution.py:83
  106.3 238.7 %all-reduce.10.cloned.1.call-start = ((), (), s32[]{:S(2)}) async-start(), calls=%async_computation.7 | async-start | bytes 9437184 | tf_op jit(solution)/shard_map/psum | solution.py:83
  211.6 8.5 %copy-start.2 = (f32[1,768,768]{2,1,0:T(8,128)S(1)}, f32[1,768,768]{2,1,0:T(8,128)}, u32[]{:S(2)}) copy-start(f32[1,768,768]{2,1,0:T(8,128)} %get-tuple-element.18) | copy-start | bytes 7077892
  221.9 3.5 copy-start.6
  236.9 241.4 %all-reduce.8.cloned.1.call-start = ((), (), s32[]{:S(2)}) async-start(), calls=%async_computation.6 | async-start | bytes 9437184 | tf_op jit(solution)/shard_map/psum | solution.py:83
  345.1 8.5 %copy-start.3 = (f32[1,768,768]{2,1,0:T(8,128)S(1)}, f32[1,768,768]{2,1,0:T(8,128)}, u32[]{:S(2)}) copy-start(f32[1,768,768]{2,1,0:T(8,128)} %get-tuple-element.16) | copy-start | bytes 7077892
  355.4 3.5 copy-start.7
  370.2 172.5 %all-gather.3.cloned.1.call-start = ((), (), s32[]{:S(2)}) async-start(), calls=%async_computation.4 | async-start | bytes 2506752 | tf_op jit(solution)/shard_map/all_gather | solution.py:95
  478.3 8.5 %copy-start.4 = (f32[1,768,768]{2,1,0:T(8,128)S(1)}, f32[1,768,768]{2,1,0:T(8,128)}, u32[]{:S(2)}) copy-start(f32[1,768,768]{2,1,0:T(8,128)} %get-tuple-element.14) | copy-start | bytes 7077892
  486.9 13.6 %copy-start.5 = (f32[1,768,768]{2,1,0:T(8,128)S(1)}, f32[1,768,768]{2,1,0:T(8,128)}, u32[]{:S(2)}) copy-start(f32[1,768,768]{2,1,0:T(8,128)} %get-tuple-element.15) | copy-start | bytes 7077892
  500.2 106.9 %all-gather.5.cloned.1.call-start = ((), (), s32[]{:S(2)}) async-start(), calls=%async_computation.5 | async-start | bytes 6684672 | tf_op jit(solution)/shard_map/all_gather | solution.py:96
  508.2 12.5 %copy-start.8 = (f32[1,8,16,768]{3,2,1,0:T(8,128)S(1)}, f32[1,8,16,768]{3,2,1,0:T(8,128)}, u32[]{:S(2)}) copy-start(f32[1,8,16,768]{3,2,1,0:T(8,128)} %get-tuple-element.20) | copy-start | bytes 1179652
  607.1 6.0 copy-start.1
Sparse Core Ops, SparseCore 0:
  106.5 105.0 all-reduce.11
  237.0 107.9 all-reduce.9
  370.3 107.9 all-reduce.7
  500.3 42.3 all-gather.2
  545.3 61.8 all-gather.4
where the time goes:
time: 625 us; the launch traced here: 620 us
  waiting for transfers between devices  411 us (66%)
  blocking collectives  90.2 us (14%)
  matrix products  75.2 us (12%)
  between operations  14.3 us (2%)
  local copies, waits for them, and re-layouts  13.7 us (2%)
  starting transfers between devices  9.07 us (1%)
  other arithmetic  6.42 us (1%)
    psum x3, waiting for transfers between devices, shards(): gram_square, gram_wide = lax.psum((part_square, part_wide), 'tensor')  321 us
    psum x1, blocking collectives, shards(): lax.psum((squares(look_square), squares(look_wide)), ('shard', 'tensor'))  68.6 us
    all_gather x1, waiting for transfers between devices, shards(): lax.all_gather(back_wide, 'tensor', axis=1, tiled=True)  60.6 us
    dot_general x6, matrix products, polynomial(): jnp.einsum('mcd,mde->mce', row_gram, whole_gram, precision=lax.Precision....  44 us
    all_gather x1, waiting for transfers between devices, shards(): lax.all_gather(back_square, 'tensor', axis=1, tiled=True)  21 us
    dot_general x6, matrix products, partial_gram(): jnp.einsum('mrc,mrd->mcd', current, current, precision=lax.Precision.HIGH...  20.8 us
  transfers between devices with their start and end apart: 7, of which 7 were waited for; matrix products, arithmetic and copies ran while one was open for 3% of the time, Pallas kernels for 0%

commit v1 on v0

--- a/solution.py
+++ b/solution.py
@@ -92,7 +92,12 @@
         lax.all_to_all(scaled_wide, "shard", split_axis=1, concat_axis=0, tiled=True),
     )
     update_square, update_wide = (
-        lax.all_gather(back_square, "tensor", axis=1, tiled=True),
+        jnp.concatenate(
+            lax.all_to_all(
+                jnp.stack(lax.axis_size("tensor") * [back_square], axis=0), "tensor", 0, 0
+            ),
+            axis=1,
+        ),
         lax.all_gather(back_wide, "tensor", axis=1, tiled=True),
     )
     return (

time: 625 us -> 600 us (0.960)
  waiting for transfers between devices: 411 us -> 381 us
    all_gather x1, waiting for transfers between devices: 60.6 us -> 7.85 us  [shards(): lax.all_gather(back_wide, 'tensor', axis=1, tiled=True)]
    all_to_all x0 -> x1, waiting for transfers between devices: none -> 44 us  [shards(): lax.all_to_all(jnp.stack(lax.axis_size('tensor') * [back_square], axis=0)...]
    all_gather x1 -> x0, waiting for transfers between devices: 21 us -> none  [shards(): lax.all_gather(back_square, 'tensor', axis=1, tiled=True)]
where the time goes in v1:
time: 600 us; the launch traced here: 595 us
  waiting for transfers between devices  381 us (64%)
  blocking collectives  90.6 us (15%)
  matrix products  75.2 us (13%)
  between operations  14.2 us (2%)
  starting transfers between devices  14 us (2%)
  local copies, waits for them, and re-layouts  13 us (2%)
  other arithmetic  6.42 us (1%)
    psum x3, waiting for transfers between devices, shards(): gram_square, gram_wide = lax.psum((part_square, part_wide), 'tensor')  321 us
    psum x1, blocking collectives, shards(): lax.psum((squares(look_square), squares(look_wide)), ('shard', 'tensor'))  68.6 us
    all_to_all x1, waiting for transfers between devices, shards(): lax.all_to_all(jnp.stack(lax.axis_size('tensor') * [back_square], axis=0)...  44 us
    dot_general x6, matrix products, polynomial(): jnp.einsum('mcd,mde->mce', row_gram, whole_gram, precision=lax.Precision....  44 us
    dot_general x6, matrix products, partial_gram(): jnp.einsum('mrc,mrd->mcd', current, current, precision=lax.Precision.HIGH...  20.8 us
    all_to_all x1, blocking collectives, shards(): lax.all_to_all(scaled_wide, 'shard', split_axis=1, concat_axis=0, tiled=T...  13.3 us
  transfers between devices with their start and end apart: 7, of which 7 were waited for; matrix products, arithmetic and copies ran while one was open for 3% of the time, Pallas kernels for 0%

profile of v1, /device:TPU:1, one launch (start us, length us, event | category | flops | bytes accessed | tf_op | source)
XLA Modules:
  0.0 594.7 jit_solution(5053911821625027159)
XLA Ops:
  11.3 68.6 %all-reduce = (f32[8]{0:T(128)S(1)}, f32[8]{0:T(128)S(1)}) all-reduce(f32[8]{0:T(128)S(1)} %get-tuple-element.27, f32[8]{0:T(128)S(1)} %multiply_reduce_fusion), channel_id=1, replica_groups=mesh['shard'=8,'tensor'=16] {'shard','tensor'}, use_global_device_ids=true, to_apply=%region_1.0 | all-reduce | flops 16 | bytes 128 | tf_op jit(solution)/shard_map/psum | solution.py:71
  80.7 4.2 all-to-all-start
  84.9 2.0 fusion.78
  86.9 3.9 all-to-all-done
  90.8 4.3 all-to-all-start.3
  95.1 3.5 convolution_bitcast_fusion
  98.6 4.2 all-to-all-done.3
  102.9 3.5 convolution_bitcast_fusion.3
  106.6 105.0 %all-reduce.12.cloned.1.call-done = (f32[1,768,768]{2,1,0:T(8,128)}, f32[1,768,768]{2,1,0:T(8,128)}) async-done(((f32[1,768,768]{2,1,0:T(8,128)}, f32[1,768,768]{2,1,0:T(8,128)}), (f32[1,768,768]{2,1,0:T(8,128)}, f32[1,768,768]{2,1,0:T(8,128)})) %all-reduce.12.cloned.1.call-update) | async-done | bytes 4718608 | tf_op jit(solution)/shard_map/psum | solution.py:83
  211.6 8.5 %fusion.22 = f32[768,768]{1,0:T(8,128)S(1)} fusion(f32[1,768,768]{2,1,0:T(8,128)} %get-tuple-element.22), kind=kOutput, calls=%fused_computation.28 | convolution fusion | flops 5435817984 | bytes 4718592 | tf_op jit(solution)/shard_map/mcd,mde->mce/dot_general | solution.py:18
  220.1 1.8 fusion.63
  221.9 3.5 convolution_bitcast_fusion.5
  225.3 6.4 %fusion.10 = f32[768,768]{1,0:T(8,128)S(1)} fusion(f32[1,768,768]{2,1,0:T(8,128)S(1)} %copy-done.5), kind=kOutput, calls=%fused_computation.13 | convolution fusion | flops 5435817984 | bytes 4718592 | tf_op jit(solution)/shard_map/mcd,mde->mce/dot_general | solution.py:18
  233.4 3.5 convolution_bitcast_fusion.2
  237.0 108.1 %all-reduce.10.cloned.1.call-done = (f32[1,768,768]{2,1,0:T(8,128)}, f32[1,768,768]{2,1,0:T(8,128)}) async-done(((f32[1,768,768]{2,1,0:T(8,128)}, f32[1,768,768]{2,1,0:T(8,128)}), (f32[1,768,768]{2,1,0:T(8,128)}, f32[1,768,768]{2,1,0:T(8,128)})) %all-reduce.10.cloned.1.call-update) | async-done | bytes 4718608 | tf_op jit(solution)/shard_map/psum | solution.py:83
  345.0 8.5 %fusion.18 = f32[768,768]{1,0:T(8,128)S(1)} fusion(f32[1,768,768]{2,1,0:T(8,128)} %get-tuple-element.20), kind=kOutput, calls=%fused_computation.23 | convolution fusion | flops 5435817984 | bytes 4718592 | tf_op jit(solution)/shard_map/mcd,mde->mce/dot_general | solution.py:18
  353.6 1.8 fusion.66
  355.4 3.5 convolution_bitcast_fusion.4
  358.8 6.2 %fusion.6 = f32[768,768]{1,0:T(8,128)S(1)} fusion(f32[1,768,768]{2,1,0:T(8,128)S(1)} %copy-done.6), kind=kOutput, calls=%fused_computation.8 | convolution fusion | flops 5435817984 | bytes 4718592 | tf_op jit(solution)/shard_map/mcd,mde->mce/dot_general | solution.py:18
  366.7 3.5 convolution_bitcast_fusion.1
  370.2 108.1 %all-reduce.8.cloned.1.call-done = (f32[1,768,768]{2,1,0:T(8,128)}, f32[1,768,768]{2,1,0:T(8,128)}) async-done(((f32[1,768,768]{2,1,0:T(8,128)}, f32[1,768,768]{2,1,0:T(8,128)}), (f32[1,768,768]{2,1,0:T(8,128)}, f32[1,768,768]{2,1,0:T(8,128)})) %all-reduce.8.cloned.1.call-update) | async-done | bytes 4718608 | tf_op jit(solution)/shard_map/psum | solution.py:83
  478.3 8.5 %fusion.2 = f32[768,768]{1,0:T(8,128)S(1)} fusion(f32[1,768,768]{2,1,0:T(8,128)} %get-tuple-element.19), kind=kOutput, calls=%fused_computation.3 | convolution fusion | flops 5435817984 | bytes 4718592 | tf_op jit(solution)/shard_map/mcd,mde->mce/dot_general | solution.py:18
  486.8 1.7 fusion.48
  488.9 13.3 %all_to_all.50 = f32[1,128,768]{2,0,1:T(1,128)S(1)} all-to-all(f32[1,128,768]{2,0,1:T(1,128)S(1)} %copy.23), channel_id=1, replica_groups=mesh['shard'=8,'tensor'=16] {'shard'}, dimensions={1} | all-to-all | bytes 786432 | tf_op jit(solution)/shard_map/all_to_all | solution.py:92
  503.0 6.0 %fusion.14 = f32[768,768]{1,0:T(8,128)S(1)} fusion(f32[1,768,768]{2,1,0:T(8,128)S(1)} %copy-done.2), kind=kOutput, calls=%fused_computation.18 | convolution fusion | flops 5435817984 | bytes 4718592 | tf_op jit(solution)/shard_map/mcd,mde->mce/dot_general | solution.py:18
  509.0 1.8 fusion.75
  511.0 8.6 %all_to_all.51 = f32[1,48,768]{2,0,1:T(1,128)S(1)} all-to-all(f32[1,48,768]{2,0,1:T(1,128)S(1)} %copy.21), channel_id=1, replica_groups=mesh['shard'=8,'tensor'=16] {'shard'}, dimensions={1} | all-to-all | bytes 294912 | tf_op jit(solution)/shard_map/all_to_all | solution.py:91
  521.7 5.2 all-to-all-start.2
  527.9 44.0 %all-to-all-done.2 = f32[16,8,6,768]{3,1,2,0:T(8,128)S(1)} async-done(((f32[16,8,6,768]{3,1,2,0:T(8,128)}), f32[16,8,6,768]{3,1,2,0:T(8,128)S(1)}, u32[]{:S(2)}, u32[]{:S(2)}) %all-to-all-start.2) | async-done | bytes 2359328 | tf_op jit(solution)/shard_map/all_to_all | solution.py:96
  572.0 2.1 copy.24
  574.1 7.8 %all-gather.2.cloned.1.call-done = f32[8,256,768]{2,1,0:T(8,128)} async-done(((f32[8,16,768]{2,1,0:T(8,128)}), f32[8,256,768]{2,1,0:T(8,128)}) %all-gather.2.cloned.1.call-update) | async-done | bytes 6291472 | tf_op jit(solution)/shard_map/all_gather | solution.py:101
  581.9 6.0 %copy.53 = f32[8,256,768]{2,1,0:T(8,128)} copy(f32[8,256,768]{2,1,0:T(8,128)} %all-gather.2.cloned.1.call-done) | data formatting | bytes 12582912
  (45 shorter events, 13.0 us)
Async XLA Ops:
  7.2 2.1 copy-start
  80.7 10.1 %all-to-all-start = ((f32[8,6,768]{2,1,0:T(8,128)}), f32[8,6,768]{2,1,0:T(8,128)S(1)}, u32[]{:S(2)}, u32[]{:S(2)}) async-start(f32[8,6,768]{2,1,0:T(8,128)} %copy.20), calls=%async_computation | async-start | bytes 393216 | tf_op jit(solution)/shard_map/all_to_all | solution.py:77
  90.8 12.0 %all-to-all-start.3 = ((f32[8,16,768]{2,1,0:T(8,128)}), f32[8,16,768]{2,1,0:T(8,128)S(1)}, u32[]{:S(2)}, u32[]{:S(2)}) async-start(f32[8,16,768]{2,1,0:T(8,128)} %get-tuple-element.25), calls=%async_computation.3 | async-start | bytes 786432 | tf_op jit(solution)/shard_map/all_to_all | solution.py:78
  95.1 116.4 %all-reduce.12.cloned.1.call-start = ((), (), s32[]{:S(2)}) async-start(), calls=%async_computation.8 | async-start | bytes 9437184 | tf_op jit(solution)/shard_map/psum | solution.py:83
  106.3 238.7 %all-reduce.10.cloned.1.call-start = ((), (), s32[]{:S(2)}) async-start(), calls=%async_computation.7 | async-start | bytes 9437184 | tf_op jit(solution)/shard_map/psum | solution.py:83
  211.6 8.5 %copy-start.3 = (f32[1,768,768]{2,1,0:T(8,128)S(1)}, f32[1,768,768]{2,1,0:T(8,128)}, u32[]{:S(2)}) copy-start(f32[1,768,768]{2,1,0:T(8,128)} %get-tuple-element.22) | copy-start | bytes 7077892
  221.9 3.5 copy-start.5
  236.9 241.4 %all-reduce.8.cloned.1.call-start = ((), (), s32[]{:S(2)}) async-start(), calls=%async_computation.6 | async-start | bytes 9437184 | tf_op jit(solution)/shard_map/psum | solution.py:83
  345.0 8.5 %copy-start.4 = (f32[1,768,768]{2,1,0:T(8,128)S(1)}, f32[1,768,768]{2,1,0:T(8,128)}, u32[]{:S(2)}) copy-start(f32[1,768,768]{2,1,0:T(8,128)} %get-tuple-element.20) | copy-start | bytes 7077892
  355.3 3.5 copy-start.6
  370.1 211.8 %all-gather.2.cloned.1.call-start = ((), (), s32[]{:S(2)}) async-start(), calls=%async_computation.5 | async-start | bytes 6684672 | tf_op jit(solution)/shard_map/all_gather | solution.py:101
  478.3 8.5 %copy-start.7 = (f32[1,768,768]{2,1,0:T(8,128)S(1)}, f32[1,768,768]{2,1,0:T(8,128)}, u32[]{:S(2)}) copy-start(f32[1,768,768]{2,1,0:T(8,128)} %get-tuple-element.19) | copy-start | bytes 7077892
  488.5 14.5 %copy-start.2 = (f32[1,768,768]{2,1,0:T(8,128)S(1)}, f32[1,768,768]{2,1,0:T(8,128)}, u32[]{:S(2)}) copy-start(f32[1,768,768]{2,1,0:T(8,128)} %get-tuple-element.18) | copy-start | bytes 7077892
  521.7 5.2 copy-start.8
  521.7 50.2 %all-to-all-start.2 = ((f32[16,8,6,768]{3,1,2,0:T(8,128)}), f32[16,8,6,768]{3,1,2,0:T(8,128)S(1)}, u32[]{:S(2)}, u32[]{:S(2)}) async-start(f32[16,8,6,768]{3,1,2,0:T(8,128)} %stack.5), calls=%async_computation.2 | async-start | bytes 4718592 | tf_op jit(solution)/shard_map/all_to_all | solution.py:96
  581.9 6.0 %copy-start.1 = (bf16[8,96,768]{2,1,0:T(8,128)(2,1)S(1)}, bf16[8,96,768]{2,1,0:T(8,128)(2,1)}, u32[]{:S(2)}) copy-start(bf16[8,96,768]{2,1,0:T(8,128)(2,1)} %param.4) | copy-start | bytes 3538948
Sparse Core Ops, SparseCore 0:
  106.5 105.0 all-reduce.11
  237.0 107.9 all-reduce.9
  370.3 107.9 all-reduce.7
  503.1 78.7 all-gather.1
